TPU v7x, 128 devices: a whole 4x4x4 slice. The times are simulated.
128 devices in a mesh: row: 64 (over y, z, x_lo, core), rep: 2 (over x_hi).
Axes of the slice: x: 4 (x_hi: 2, x_lo: 2; x = x_hi * 2 + x_lo), y: 4, z: 4, core: 2. Of those that a mesh axis runs over, the one named last changes fastest.
Arguments:
- out_grad: bfloat16 [65536, 256], P(('row', 'rep')), may hold values from -6 to 6
- relu_mask: int32 [65536, 256], P(('row', 'rep')), may hold values 0 or 1
- features: bfloat16 [65536, 256], P('row'), may hold values from -6 to 6
- weight: bfloat16 [256, 256], replicated, may hold values from -0.375 to 0.375
- tile_cols: int32 [512, 128], P('row', 'rep'), may hold values from 0 to 255, as said below
- tile_counts: int32 [512, 2], P('row', 'rep'), may hold values from 1 to 64
- tile_values: bfloat16 [512, 128, 128, 128], P('row', 'rep')
Outputs:
- grad_in: bfloat16 [65536, 256], P(('row', 'rep'))
- grad_weight: float32 [256, 256], replicated
Inputs may be any that keep to these rules, and one draw needn't show every extreme that they name: `tile_cols`: the 64 entries of one row tile and one index of rep are distinct column tiles.
All inputs are finite; a program needn't handle non-finite values. No bound on the sum of `relu_mask` on one device may be relied on, other than what follows from the above.
Results may differ from a plain program's by a relative error of at most 0.0049.
Values may be sent and summed in bfloat16 or wider, within the bound.
No kernel may reach another device: no remote copies, remote signals or barrier semaphores. Data moves between devices by JAX's collectives and lax.ppermute only.
A program may use at most 320 MiB of HBM per device.

v0:
```python
import math
import jax
import jax.numpy as jnp
from jax import lax
from jax.sharding import PartitionSpec as P

AXES = ("row", "rep")
CORE_BIT = 1
DOUBLING_STAGES = ((2, 0), (3, 4), (5, 6))


def xor_pairs(count, mask):
    return [(i, i ^ mask) for i in range(count)]


def group_mask(d, bits):
    return sum(((d >> i & 1) << b for i, b in enumerate(bits)))


def group_pos(idx, bits):
    return sum(((idx >> b & 1) << i for i, b in enumerate(bits)))


def butterfly_sum(x):
    count = lax.axis_size("row") * lax.axis_size("rep")
    idx = lax.axis_index(AXES)
    core = idx >> CORE_BIT & 1
    core_mask = 1 << CORE_BIT
    parts = x.reshape(2, x.shape[0] // 2, *x.shape[1:])
    mine = jnp.take(parts, core, axis=0)
    other = lax.ppermute(jnp.take(parts, 1 - core, axis=0), AXES, xor_pairs(count, core_mask))
    buf = jnp.where(core == 0, mine + other, other + mine)
    for bits in DOUBLING_STAGES:
        m = 1 << len(bits)
        pos = group_pos(idx, bits)
        got = [buf] + [
            lax.ppermute(buf, AXES, xor_pairs(count, group_mask(d, bits))) for d in range(1, m)
        ]
        ordered = jnp.take(jnp.stack(got), jnp.arange(m, dtype=jnp.int32) ^ pos, axis=0)
        buf = ordered[0]
        for j in range(1, m):
            buf = buf + ordered[j]
    got = lax.ppermute(buf, AXES, xor_pairs(count, core_mask))
    return jnp.where(core == 0, jnp.concatenate([buf, got]), jnp.concatenate([got, buf]))


def shards(out_grad, relu_mask, features, weight, tile_cols, tile_counts, tile_values):
    own_rows, feature_width = out_grad.shape
    row_tiles, most_slots = tile_cols.shape
    tile_size = tile_values.shape[-1]
    block_tiles = own_rows // tile_size
    column_tiles = block_tiles * lax.axis_size("row")
    gated = out_grad * relu_mask.astype(jnp.bfloat16)
    active = jnp.arange(most_slots, dtype=jnp.int32)[None, :] < tile_counts
    gathered = lax.all_gather(gated, "row", axis=0, tiled=True)
    grad_tiles = gathered.reshape(column_tiles, tile_size, feature_width)
    picked = jnp.take(grad_tiles, tile_cols, axis=0)
    picked = jnp.where(active[:, :, None, None], picked, jnp.zeros((), jnp.bfloat16))
    partial_sum = jnp.einsum(
        "tsab,tsbf->taf", tile_values, picked, preferred_element_type=jnp.float32
    )
    partial_sum = partial_sum.reshape(row_tiles * tile_size, feature_width)
    node_count = own_rows * lax.axis_size("row") * lax.axis_size("rep")
    normalizer = 1.0 / math.sqrt(node_count)
    weight_term = jnp.dot(
        features.astype(jnp.float32).T, partial_sum, precision=lax.Precision.HIGHEST
    )
    grad_weight = butterfly_sum(weight_term * normalizer)
    rep = lax.axis_index("rep")
    halves = partial_sum.reshape(2, own_rows, feature_width)
    other = lax.ppermute(jnp.take(halves, 1 - rep, axis=0), "rep", [(0, 1), (1, 0)])
    propagated = jnp.take(halves, rep, axis=0) + other
    grad_in = jnp.dot(
        propagated.astype(jnp.bfloat16), weight.T, preferred_element_type=jnp.float32
    ).astype(jnp.bfloat16)
    return (grad_in, grad_weight)


def solution(mesh):
    in_specs = (
        P(("row", "rep"), None),
        P(("row", "rep"), None),
        P("row", None),
        P(),
        P("row", "rep"),
        P("row", "rep"),
        P("row", "rep", None, None),
    )
    out_specs = (P(("row", "rep"), None), P())
    return jax.shard_map(shards, mesh=mesh, in_specs=in_specs, out_specs=out_specs, check_vma=False)
```

profile of v0, /device:TPU:1, one launch (start us, length us, event | category | flops | bytes accessed | tf_op | source)
XLA Modules:
  0.0 218.2 jit_solution(8378743402661240332)
XLA Ops:
  7.2 0.0 copy-start
  7.2 0.0 all-gather.2.cloned.1.call-start
  7.2 1.9 convert_multiply_fusion
  9.1 0.0 all-gather.2.cloned.1.call-update
  9.2 0.7 compare_select_fusion
  9.9 0.1 reshape.175
  10.0 0.8 iota_compare_fusion
  10.8 125.0 %all-gather.2.cloned.1.call-done = bf16[32768,256]{1,0:T(8,128)(2,1)} async-done(((bf16[512,256]{1,0:T(8,128)(2,1)}), bf16[32768,256]{1,0:T(8,128)(2,1)}) %all-gather.2.cloned.1.call-update) | async-done | bytes 16777232 | tf_op jit(solution)/shard_map/all_gather | solution.py:55
  135.8 21.9 %gather_fusion = bf16[512,128,256]{2,1,0:T(8,128)(2,1)} fusion(bf16[256,128,256]{2,1,0:T(8,128)(2,1)} %bitcast.45, s32[1024]{0:T(1024)S(1)} %pad_clamp_fusion.3), kind=kCustom, calls=%fused_computation.3 | custom fusion | bytes 67110912 | tf_op jit(solution)/shard_map/jit(_take)/gather | solution.py:57
  157.7 0.0 copy-start.1
  157.7 17.5 %fusion = f32[8,256,128,1]{1,2,3,0:T(8,128)S(1)} fusion(bf16[8,64,128,128]{3,2,1,0:T(8,128)(2,1)} %param.19, bf16[8,64,128,256]{3,2,1,0:T(8,128)(2,1)} %bitcast.46, pred[8,64]{1,0:T(8,128)(4,1)S(1)} %get-tuple-element.28, pred[8,64]{1,0:T(8,128)(4,1)S(1)} %get-tuple-element.27), kind=kOutput, calls=%fused_computation.4 | convolution fusion | flops 4328521728 | bytes 51381248 | tf_op jit(solution)/shard_map/tsab,tsbf->taf/dot_general | solution.py:59
  175.2 0.0 copy-done
  175.2 0.8 convolution_multiply_fusion
  176.1 0.4 collective-permute-start.1
  176.4 1.0 collective-permute-done.1
  177.5 1.9 collective-permute-start.4
  179.4 0.6 collective-permute-start.3
  180.0 0.8 collective-permute-start.2
  180.9 2.3 %collective-permute-start = (f32[512,256]{1,0:T(8,128)S(1)}, f32[512,256]{1,0:T(8,128)}, u32[]{:S(2)}, u32[]{:S(2)}) collective-permute-start(f32[512,256]{1,0:T(8,128)S(1)} %select_bitcast_fusion), channel_id=1, source_target_pairs={{0,1},{1,0},{2,3},{3,2},{4,5},{5,4},{6,7},{7,6},{8,9},{9,8},{10,11... | collective-permute-start | bytes 1572872 | tf_op jit(solution)/shard_map/ppermute | solution.py:71
  183.2 1.1 collective-permute-done.4
  184.2 1.3 collective-permute-done.3
  185.5 1.3 collective-permute-done.2
  186.8 0.6 gather_fusion.1
  187.4 0.1 broadcast_select_fusion.2
  187.6 1.3 collective-permute-start.7
  188.9 1.3 collective-permute-start.6
  190.2 0.8 collective-permute-start.5
  190.9 2.1 collective-permute-done.7
  193.1 1.5 collective-permute-done.6
  194.6 0.5 collective-permute-done.5
  195.1 0.6 gather_fusion.2
  195.7 0.1 broadcast_select_fusion.1
  195.8 1.4 collective-permute-start.10
  197.3 1.0 collective-permute-start.9
  198.3 0.9 collective-permute-start.8
  199.2 1.7 collective-permute-done.10
  201.0 1.6 collective-permute-done.9
  202.6 0.4 collective-permute-done.8
  203.0 0.6 gather_fusion.3
  203.6 0.1 broadcast_select_fusion
  203.7 4.9 %collective-permute-start.11 = (f32[128,256]{1,0:T(8,128)S(1)}, f32[128,256]{1,0:T(8,128)S(1)}, u32[]{:S(2)}, u32[]{:S(2)}) collective-permute-start(f32[128,256]{1,0:T(8,128)S(1)} %fusion.11), channel_id=1, source_target_pairs={{0,2},{1,3},{2,0},{3,1},{4,6},{5,7},{6,4},{7,5},{8,10},{9,11},{10,... | collective-permute-start | bytes 393224 | tf_op jit(solution)/shard_map/ppermute | solution.py:43
  208.6 0.0 collective-permute-done
  208.6 0.0 copy-done.1
  208.6 2.0 convolution_convert_fusion
  210.6 0.0 collective-permute-done.11
  210.6 0.7 maximum_select_fusion
  (20 shorter events, 0.4 us)
Async XLA Ops:
  7.2 168.1 %copy-start = (bf16[1024,256]{1,0:T(8,128)(2,1)S(1)}, bf16[1024,256]{1,0:T(8,128)(2,1)}, u32[]{:S(2)}) copy-start(bf16[1024,256]{1,0:T(8,128)(2,1)} %param.15) | copy-start | bytes 1572868
  7.2 128.6 %all-gather.2.cloned.1.call-start = ((), (), s32[]{:S(2)}) async-start(), calls=%async_computation | async-start | bytes 17039360 | tf_op jit(solution)/shard_map/all_gather | solution.py:55
  157.7 50.9 %copy-start.1 = (bf16[256,256]{1,0:T(8,128)(2,1)S(1)}, bf16[256,256]{1,0:T(8,128)(2,1)}, u32[]{:S(2)}) copy-start(bf16[256,256]{1,0:T(8,128)(2,1)} %param.16) | copy-start | bytes 393220
  176.1 1.4 collective-permute-start.1
  177.5 6.7 %collective-permute-start.4 = (f32[128,256]{1,0:T(8,128)S(1)}, f32[128,256]{1,0:T(8,128)S(1)}, u32[]{:S(2)}, u32[]{:S(2)}) collective-permute-start(f32[128,256]{1,0:T(8,128)S(1)} %bitcast_add_fusion.1), channel_id=1, source_target_pairs={{0,5},{1,4},{2,7},{3,6},{4,1},{5,0},{6,3},{7,2},{8,13},{9,12},{10,... | collective-permute-start | bytes 393224 | tf_op jit(solution)/shard_map/ppermute | solution.py:37
  179.4 6.1 %collective-permute-start.3 = (f32[128,256]{1,0:T(8,128)S(1)}, f32[128,256]{1,0:T(8,128)S(1)}, u32[]{:S(2)}, u32[]{:S(2)}) collective-permute-start(f32[128,256]{1,0:T(8,128)S(1)} %bitcast_add_fusion.1), channel_id=1, source_target_pairs={{0,1},{1,0},{2,3},{3,2},{4,5},{5,4},{6,7},{7,6},{8,9},{9,8},{10,11... | collective-permute-start | bytes 393224 | tf_op jit(solution)/shard_map/ppermute | solution.py:37
  180.0 6.8 %collective-permute-start.2 = (f32[128,256]{1,0:T(8,128)S(1)}, f32[128,256]{1,0:T(8,128)S(1)}, u32[]{:S(2)}, u32[]{:S(2)}) collective-permute-start(f32[128,256]{1,0:T(8,128)S(1)} %bitcast_add_fusion.1), channel_id=1, source_target_pairs={{0,4},{1,5},{2,6},{3,7},{4,0},{5,1},{6,2},{7,3},{8,12},{9,13},{10,... | collective-permute-start | bytes 393224 | tf_op jit(solution)/shard_map/ppermute | solution.py:37
  180.9 27.7 %collective-permute-start = (f32[512,256]{1,0:T(8,128)S(1)}, f32[512,256]{1,0:T(8,128)}, u32[]{:S(2)}, u32[]{:S(2)}) collective-permute-start(f32[512,256]{1,0:T(8,128)S(1)} %select_bitcast_fusion), channel_id=1, source_target_pairs={{0,1},{1,0},{2,3},{3,2},{4,5},{5,4},{6,7},{7,6},{8,9},{9,8},{10,11... | collective-permute-start | bytes 1572872 | tf_op jit(solution)/shard_map/ppermute | solution.py:71
  187.6 5.5 %collective-permute-start.7 = (f32[128,256]{1,0:T(8,128)S(1)}, f32[128,256]{1,0:T(8,128)S(1)}, u32[]{:S(2)}, u32[]{:S(2)}) collective-permute-start(f32[128,256]{1,0:T(8,128)S(1)} %fusion.21), channel_id=1, source_target_pairs={{0,24},{1,25},{2,26},{3,27},{4,28},{5,29},{6,30},{7,31},{8,16},{9,... | collective-permute-start | bytes 393224 | tf_op jit(solution)/shard_map/ppermute | solution.py:37
  188.9 5.7 %collective-permute-start.6 = (f32[128,256]{1,0:T(8,128)S(1)}, f32[128,256]{1,0:T(8,128)S(1)}, u32[]{:S(2)}, u32[]{:S(2)}) collective-permute-start(f32[128,256]{1,0:T(8,128)S(1)} %fusion.21), channel_id=1, source_target_pairs={{0,16},{1,17},{2,18},{3,19},{4,20},{5,21},{6,22},{7,23},{8,24},{9,... | collective-permute-start | bytes 393224 | tf_op jit(solution)/shard_map/ppermute | solution.py:37
  190.2 4.9 %collective-permute-start.5 = (f32[128,256]{1,0:T(8,128)S(1)}, f32[128,256]{1,0:T(8,128)S(1)}, u32[]{:S(2)}, u32[]{:S(2)}) collective-permute-start(f32[128,256]{1,0:T(8,128)S(1)} %fusion.21), channel_id=1, source_target_pairs={{0,8},{1,9},{2,10},{3,11},{4,12},{5,13},{6,14},{7,15},{8,0},{9,1},... | collective-permute-start | bytes 393224 | tf_op jit(solution)/shard_map/ppermute | solution.py:37
  195.8 5.1 %collective-permute-start.10 = (f32[128,256]{1,0:T(8,128)S(1)}, f32[128,256]{1,0:T(8,128)S(1)}, u32[]{:S(2)}, u32[]{:S(2)}) collective-permute-start(f32[128,256]{1,0:T(8,128)S(1)} %fusion.20), channel_id=1, source_target_pairs={{0,96},{1,97},{2,98},{3,99},{4,100},{5,101},{6,102},{7,103},{8,104... | collective-permute-start | bytes 393224 | tf_op jit(solution)/shard_map/ppermute | solution.py:37
  197.3 5.3 %collective-permute-start.9 = (f32[128,256]{1,0:T(8,128)S(1)}, f32[128,256]{1,0:T(8,128)S(1)}, u32[]{:S(2)}, u32[]{:S(2)}) collective-permute-start(f32[128,256]{1,0:T(8,128)S(1)} %fusion.20), channel_id=1, source_target_pairs={{0,64},{1,65},{2,66},{3,67},{4,68},{5,69},{6,70},{7,71},{8,72},{9,... | collective-permute-start | bytes 393224 | tf_op jit(solution)/shard_map/ppermute | solution.py:37
  198.3 4.6 %collective-permute-start.8 = (f32[128,256]{1,0:T(8,128)S(1)}, f32[128,256]{1,0:T(8,128)S(1)}, u32[]{:S(2)}, u32[]{:S(2)}) collective-permute-start(f32[128,256]{1,0:T(8,128)S(1)} %fusion.20), channel_id=1, source_target_pairs={{0,32},{1,33},{2,34},{3,35},{4,36},{5,37},{6,38},{7,39},{8,40},{9,... | collective-permute-start | bytes 393224 | tf_op jit(solution)/shard_map/ppermute | solution.py:37
  203.7 6.9 %collective-permute-start.11 = (f32[128,256]{1,0:T(8,128)S(1)}, f32[128,256]{1,0:T(8,128)S(1)}, u32[]{:S(2)}, u32[]{:S(2)}) collective-permute-start(f32[128,256]{1,0:T(8,128)S(1)} %fusion.11), channel_id=1, source_target_pairs={{0,2},{1,3},{2,0},{3,1},{4,6},{5,7},{6,4},{7,5},{8,10},{9,11},{10,... | collective-permute-start | bytes 393224 | tf_op jit(solution)/shard_map/ppermute | solution.py:43
Sparse Core Ops, SparseCore 0:
  10.3 125.4 all-gather.1
where the time goes:
time: 218 us
  waiting for transfers between devices  138 us (63%)
  local copies, waits for them, and re-layouts  23.8 us (11%)
  matrix products  20.3 us (9%)
  starting transfers between devices  17.6 us (8%)
  between operations  14.2 us (7%)
  other arithmetic  4.84 us (2%)
    all_gather x1, waiting for transfers between devices, shards(): gathered = lax.all_gather(gated, 'row', axis=0, tiled=True)  125 us
    gather x1, local copies, waits for them, and re-layouts, shards(): picked = jnp.take(grad_tiles, tile_cols, axis=0)  21.9 us
    dot_general x1, matrix products, shards(): jnp.einsum('tsab,tsbf->taf', tile_values, picked, preferred_element_type=...  17.5 us
    ppermute x9, waiting for transfers between devices, butterfly_sum(): lax.ppermute(buf, AXES, xor_pairs(count, group_mask(d, bits)))  11.4 us
    ppermute x9, starting transfers between devices, butterfly_sum(): lax.ppermute(buf, AXES, xor_pairs(count, group_mask(d, bits)))  10 us
    ppermute x1, starting transfers between devices, butterfly_sum(): got = lax.ppermute(buf, AXES, xor_pairs(count, core_mask))  4.89 us
  transfers between devices with their start and end apart: 13, of which 11 were waited for; matrix products, arithmetic and copies ran while one was open for 3% of the time, Pallas kernels for 0%

commit v1 on v0

--- a/solution.py
+++ b/solution.py
@@ -52,7 +52,9 @@
     column_tiles = block_tiles * lax.axis_size("row")
     gated = out_grad * relu_mask.astype(jnp.bfloat16)
     active = jnp.arange(most_slots, dtype=jnp.int32)[None, :] < tile_counts
-    gathered = lax.all_gather(gated, "row", axis=0, tiled=True)
+    gathered = jnp.concatenate(
+        lax.all_to_all(jnp.stack([gated for _ in range(lax.axis_size("row"))]), "row", 0, 0), axis=0
+    )
     grad_tiles = gathered.reshape(column_tiles, tile_size, feature_width)
     picked = jnp.take(grad_tiles, tile_cols, axis=0)
     picked = jnp.where(active[:, :, None, None], picked, jnp.zeros((), jnp.bfloat16))

time: 218 us -> 352 us (1.61)
  waiting for transfers between devices: 138 us -> 221 us
  starting transfers between devices: 17.6 us -> 76.8 us
  between operations: 14.2 us -> 0.9 us
  local copies, waits for them, and re-layouts: 23.8 us -> 29.7 us
    all_to_all x0 -> x1, waiting for transfers between devices: none -> 207 us  [shards(): lax.all_to_all(jnp.stack([gated for _ in range(lax.axis_size('row'))]), '...]
    all_gather x1 -> x0, waiting for transfers between devices: 125 us -> none  [shards(): gathered = lax.all_gather(gated, 'row', axis=0, tiled=True)]
    ppermute x9, starting transfers between devices: 10 us -> 58.7 us  [butterfly_sum(): lax.ppermute(buf, AXES, xor_pairs(count, group_mask(d, bits)))]
    all_to_all x0 -> x1, starting transfers between devices: none -> 11.1 us  [shards(): lax.all_to_all(jnp.stack([gated for _ in range(lax.axis_size('row'))]), '...]
    another operation x0 -> x1, local copies, waits for them, and re-layouts: none -> 5.95 us  [shards(): jnp.stack([gated for _ in range(lax.axis_size('row'))])]
  transfers between devices with their start and end apart: 13 -> 13, of which waited for: 11 -> 9; matrix products, arithmetic and copies ran while one was open for 3% -> 1% of each run, Pallas kernels for 0% -> 0%
where the time goes in v1:
time: 352 us; the launch traced here: 351 us
  waiting for transfers between devices  221 us (63%)
  starting transfers between devices  76.8 us (22%)
  local copies, waits for them, and re-layouts  29.7 us (8%)
  matrix products  20.3 us (6%)
    all_to_all x1, waiting for transfers between devices, shards(): lax.all_to_all(jnp.stack([gated for _ in range(lax.axis_size('row'))]), '...  207 us
    ppermute x9, starting transfers between devices, butterfly_sum(): lax.ppermute(buf, AXES, xor_pairs(count, group_mask(d, bits)))  58.7 us
    gather x1, local copies, waits for them, and re-layouts, shards(): picked = jnp.take(grad_tiles, tile_cols, axis=0)  21.9 us
    dot_general x1, matrix products, shards(): jnp.einsum('tsab,tsbf->taf', tile_values, picked, preferred_element_type=...  17.5 us
    ppermute x9, waiting for transfers between devices, butterfly_sum(): lax.ppermute(buf, AXES, xor_pairs(count, group_mask(d, bits)))  12.8 us
    all_to_all x1, starting transfers between devices, shards(): lax.all_to_all(jnp.stack([gated for _ in range(lax.axis_size('row'))]), '...  11.1 us
  transfers between devices with their start and end apart: 13, of which 9 were waited for; matrix products, arithmetic and copies ran while one was open for 1% of the time, Pallas kernels for 0%

profile of v1, /device:TPU:1, one launch (start us, length us, event | category | flops | bytes accessed | tf_op | source)
XLA Modules:
  0.0 351.3 jit_solution(10029444392687819280)
XLA Ops:
  0.6 0.0 copy-start
  0.6 0.0 copy-start.2
  0.7 0.0 copy-start.3
  0.7 1.2 convert_multiply_fusion
  1.9 6.0 %stack.28 = bf16[64,512,256]{2,1,0:T(8,128)(2,1)} broadcast(bf16[512,256]{1,0:T(8,128)(2,1)S(1)} %convert_multiply_fusion), dimensions={1,2} | broadcast | bytes 17039360 | tf_op jit(solution)/shard_map/stack | solution.py:56
  7.8 11.1 %all-to-all-start = ((bf16[64,512,256]{2,1,0:T(8,128)(2,1)}), bf16[64,512,256]{2,1,0:T(8,128)(2,1)}, u32[]{:S(2)}, u32[]{:S(2)}) async-start(bf16[64,512,256]{2,1,0:T(8,128)(2,1)} %stack.28), calls=%async_computation | async-start | bytes 33554432 | tf_op jit(solution)/shard_map/all_to_all | solution.py:56
  19.0 0.0 copy-done.2
  19.0 0.1 reshape.173
  19.1 0.0 copy-done.3
  19.1 0.1 iota_compare_fusion
  19.2 207.0 %all-to-all-done = bf16[64,512,256]{2,1,0:T(8,128)(2,1)} async-done(((bf16[64,512,256]{2,1,0:T(8,128)(2,1)}), bf16[64,512,256]{2,1,0:T(8,128)(2,1)}, u32[]{:S(2)}, u32[]{:S(2)}) %all-to-all-start) | async-done | bytes 16777248 | tf_op jit(solution)/shard_map/all_to_all | solution.py:56
  226.2 21.9 %gather_fusion = bf16[512,128,256]{2,1,0:T(8,128)(2,1)} fusion(bf16[256,128,256]{2,1,0:T(8,128)(2,1)} %bitcast.1, s32[1024]{0:T(1024)S(1)} %pad_clamp_fusion.3), kind=kCustom, calls=%fused_computation.3 | custom fusion | bytes 67110912 | tf_op jit(solution)/shard_map/jit(_take)/gather | solution.py:59
  248.2 0.0 copy-start.1
  248.2 17.5 %fusion = f32[8,256,128,1]{1,2,3,0:T(8,128)S(1)} fusion(bf16[8,64,128,128]{3,2,1,0:T(8,128)(2,1)} %param.19, bf16[8,64,128,256]{3,2,1,0:T(8,128)(2,1)} %bitcast.45, pred[8,64]{1,0:T(8,128)(4,1)S(1)} %get-tuple-element.28, pred[8,64]{1,0:T(8,128)(4,1)S(1)} %get-tuple-element.27), kind=kOutput, calls=%fused_computation.4 | convolution fusion | flops 4328521728 | bytes 51381248 | tf_op jit(solution)/shard_map/tsab,tsbf->taf/dot_general | solution.py:61
  265.7 0.0 copy-done
  265.7 0.8 convolution_multiply_fusion
  266.5 1.2 collective-permute-start.1
  267.7 1.0 collective-permute-done.1
  268.7 38.8 %collective-permute-start.4 = (f32[128,256]{1,0:T(8,128)S(1)}, f32[128,256]{1,0:T(8,128)S(1)}, u32[]{:S(2)}, u32[]{:S(2)}) collective-permute-start(f32[128,256]{1,0:T(8,128)S(1)} %bitcast_add_fusion.1), channel_id=1, source_target_pairs={{0,5},{1,4},{2,7},{3,6},{4,1},{5,0},{6,3},{7,2},{8,13},{9,12},{10,... | collective-permute-start | bytes 393224 | tf_op jit(solution)/shard_map/ppermute | solution.py:37
  307.6 0.5 collective-permute-start.3
  308.1 0.1 collective-permute-start.2
  308.3 2.4 collective-permute-start
  310.7 2.4 collective-permute-done.4
  313.1 0.4 collective-permute-done.3
  313.5 0.8 collective-permute-done.2
  314.3 0.6 gather_fusion.1
  314.9 0.1 broadcast_select_fusion.2
  315.1 0.1 collective-permute-start.7
  315.2 15.3 %collective-permute-start.6 = (f32[128,256]{1,0:T(8,128)S(1)}, f32[128,256]{1,0:T(8,128)S(1)}, u32[]{:S(2)}, u32[]{:S(2)}) collective-permute-start(f32[128,256]{1,0:T(8,128)S(1)} %fusion.21), channel_id=1, source_target_pairs={{0,16},{1,17},{2,18},{3,19},{4,20},{5,21},{6,22},{7,23},{8,24},{9,... | collective-permute-start | bytes 393224 | tf_op jit(solution)/shard_map/ppermute | solution.py:37
  330.5 0.0 collective-permute-start.5
  330.5 0.0 collective-permute-done.7
  330.5 2.3 collective-permute-done.6
  332.8 2.5 collective-permute-done.5
  335.4 0.6 gather_fusion.2
  336.0 0.1 broadcast_select_fusion.1
  336.1 0.1 collective-permute-start.10
  336.2 3.8 %collective-permute-start.9 = (f32[128,256]{1,0:T(8,128)S(1)}, f32[128,256]{1,0:T(8,128)S(1)}, u32[]{:S(2)}, u32[]{:S(2)}) collective-permute-start(f32[128,256]{1,0:T(8,128)S(1)} %fusion.20), channel_id=1, source_target_pairs={{0,64},{1,65},{2,66},{3,67},{4,68},{5,69},{6,70},{7,71},{8,72},{9,... | collective-permute-start | bytes 393224 | tf_op jit(solution)/shard_map/ppermute | solution.py:37
  340.0 0.0 collective-permute-start.8
  340.1 2.6 collective-permute-done.10
  342.7 0.0 collective-permute-done.9
  342.7 1.7 collective-permute-done.8
  344.4 0.6 gather_fusion.3
  345.0 0.1 broadcast_select_fusion
  345.2 3.4 collective-permute-start.11
  348.6 0.0 collective-permute-done
  348.6 0.0 copy-done.1
  348.6 2.0 convolution_convert_fusion
  350.6 0.0 collective-permute-done.11
  350.6 0.7 maximum_select_fusion
  (21 shorter events, 0.4 us)
Async XLA Ops:
  0.6 265.1 %copy-start = (bf16[1024,256]{1,0:T(8,128)(2,1)S(1)}, bf16[1024,256]{1,0:T(8,128)(2,1)}, u32[]{:S(2)}) copy-start(bf16[1024,256]{1,0:T(8,128)(2,1)} %param.15) | copy-start | bytes 1572868
  0.6 18.3 %copy-start.2 = (s32[8,64]{1,0:T(8,128)S(1)}, s32[8,64]{1,0:T(8,128)}, u32[]{:S(2)}) copy-start(s32[8,64]{1,0:T(8,128)} %param.17) | copy-start | bytes 6148
  0.7 18.5 %copy-start.3 = (s32[8,1]{0,1:T(1,128)S(1)}, s32[8,1]{0,1:T(1,128)}, u32[]{:S(2)}) copy-start(s32[8,1]{0,1:T(1,128)} %param.18) | copy-start | bytes 100
  7.8 218.4 %all-to-all-start = ((bf16[64,512,256]{2,1,0:T(8,128)(2,1)}), bf16[64,512,256]{2,1,0:T(8,128)(2,1)}, u32[]{:S(2)}, u32[]{:S(2)}) async-start(bf16[64,512,256]{2,1,0:T(8,128)(2,1)} %stack.28), calls=%async_computation | async-start | bytes 33554432 | tf_op jit(solution)/shard_map/all_to_all | solution.py:56
  248.2 100.4 %copy-start.1 = (bf16[256,256]{1,0:T(8,128)(2,1)S(1)}, bf16[256,256]{1,0:T(8,128)(2,1)}, u32[]{:S(2)}) copy-start(bf16[256,256]{1,0:T(8,128)(2,1)} %param.16) | copy-start | bytes 393220
  266.5 2.2 collective-permute-start.1
  268.7 44.3 %collective-permute-start.4 = (f32[128,256]{1,0:T(8,128)S(1)}, f32[128,256]{1,0:T(8,128)S(1)}, u32[]{:S(2)}, u32[]{:S(2)}) collective-permute-start(f32[128,256]{1,0:T(8,128)S(1)} %bitcast_add_fusion.1), channel_id=1, source_target_pairs={{0,5},{1,4},{2,7},{3,6},{4,1},{5,0},{6,3},{7,2},{8,13},{9,12},{10,... | collective-permute-start | bytes 393224 | tf_op jit(solution)/shard_map/ppermute | solution.py:37
  307.6 5.9 %collective-permute-start.3 = (f32[128,256]{1,0:T(8,128)S(1)}, f32[128,256]{1,0:T(8,128)S(1)}, u32[]{:S(2)}, u32[]{:S(2)}) collective-permute-start(f32[128,256]{1,0:T(8,128)S(1)} %bitcast_add_fusion.1), channel_id=1, source_target_pairs={{0,1},{1,0},{2,3},{3,2},{4,5},{5,4},{6,7},{7,6},{8,9},{9,8},{10,11... | collective-permute-start | bytes 393224 | tf_op jit(solution)/shard_map/ppermute | solution.py:37
  308.1 6.2 %collective-permute-start.2 = (f32[128,256]{1,0:T(8,128)S(1)}, f32[128,256]{1,0:T(8,128)S(1)}, u32[]{:S(2)}, u32[]{:S(2)}) collective-permute-start(f32[128,256]{1,0:T(8,128)S(1)} %bitcast_add_fusion.1), channel_id=1, source_target_pairs={{0,4},{1,5},{2,6},{3,7},{4,0},{5,1},{6,2},{7,3},{8,12},{9,13},{10,... | collective-permute-start | bytes 393224 | tf_op jit(solution)/shard_map/ppermute | solution.py:37
  308.3 40.3 %collective-permute-start = (f32[512,256]{1,0:T(8,128)S(1)}, f32[512,256]{1,0:T(8,128)}, u32[]{:S(2)}, u32[]{:S(2)}) collective-permute-start(f32[512,256]{1,0:T(8,128)S(1)} %select_bitcast_fusion), channel_id=1, source_target_pairs={{0,1},{1,0},{2,3},{3,2},{4,5},{5,4},{6,7},{7,6},{8,9},{9,8},{10,11... | collective-permute-start | bytes 1572872 | tf_op jit(solution)/shard_map/ppermute | solution.py:73
  315.1 15.4 %collective-permute-start.7 = (f32[128,256]{1,0:T(8,128)S(1)}, f32[128,256]{1,0:T(8,128)S(1)}, u32[]{:S(2)}, u32[]{:S(2)}) collective-permute-start(f32[128,256]{1,0:T(8,128)S(1)} %fusion.21), channel_id=1, source_target_pairs={{0,24},{1,25},{2,26},{3,27},{4,28},{5,29},{6,30},{7,31},{8,16},{9,... | collective-permute-start | bytes 393224 | tf_op jit(solution)/shard_map/ppermute | solution.py:37
  315.2 17.6 %collective-permute-start.6 = (f32[128,256]{1,0:T(8,128)S(1)}, f32[128,256]{1,0:T(8,128)S(1)}, u32[]{:S(2)}, u32[]{:S(2)}) collective-permute-start(f32[128,256]{1,0:T(8,128)S(1)} %fusion.21), channel_id=1, source_target_pairs={{0,16},{1,17},{2,18},{3,19},{4,20},{5,21},{6,22},{7,23},{8,24},{9,... | collective-permute-start | bytes 393224 | tf_op jit(solution)/shard_map/ppermute | solution.py:37
  330.5 4.9 %collective-permute-start.5 = (f32[128,256]{1,0:T(8,128)S(1)}, f32[128,256]{1,0:T(8,128)S(1)}, u32[]{:S(2)}, u32[]{:S(2)}) collective-permute-start(f32[128,256]{1,0:T(8,128)S(1)} %fusion.21), channel_id=1, source_target_pairs={{0,8},{1,9},{2,10},{3,11},{4,12},{5,13},{6,14},{7,15},{8,0},{9,1},... | collective-permute-start | bytes 393224 | tf_op jit(solution)/shard_map/ppermute | solution.py:37
  336.1 6.5 %collective-permute-start.10 = (f32[128,256]{1,0:T(8,128)S(1)}, f32[128,256]{1,0:T(8,128)S(1)}, u32[]{:S(2)}, u32[]{:S(2)}) collective-permute-start(f32[128,256]{1,0:T(8,128)S(1)} %fusion.20), channel_id=1, source_target_pairs={{0,96},{1,97},{2,98},{3,99},{4,100},{5,101},{6,102},{7,103},{8,104... | collective-permute-start | bytes 393224 | tf_op jit(solution)/shard_map/ppermute | solution.py:37
  336.2 6.4 %collective-permute-start.9 = (f32[128,256]{1,0:T(8,128)S(1)}, f32[128,256]{1,0:T(8,128)S(1)}, u32[]{:S(2)}, u32[]{:S(2)}) collective-permute-start(f32[128,256]{1,0:T(8,128)S(1)} %fusion.20), channel_id=1, source_target_pairs={{0,64},{1,65},{2,66},{3,67},{4,68},{5,69},{6,70},{7,71},{8,72},{9,... | collective-permute-start | bytes 393224 | tf_op jit(solution)/shard_map/ppermute | solution.py:37
  340.0 4.4 %collective-permute-start.8 = (f32[128,256]{1,0:T(8,128)S(1)}, f32[128,256]{1,0:T(8,128)S(1)}, u32[]{:S(2)}, u32[]{:S(2)}) collective-permute-start(f32[128,256]{1,0:T(8,128)S(1)} %fusion.20), channel_id=1, source_target_pairs={{0,32},{1,33},{2,34},{3,35},{4,36},{5,37},{6,38},{7,39},{8,40},{9,... | collective-permute-start | bytes 393224 | tf_op jit(solution)/shard_map/ppermute | solution.py:37
  345.2 5.4 %collective-permute-start.11 = (f32[128,256]{1,0:T(8,128)S(1)}, f32[128,256]{1,0:T(8,128)S(1)}, u32[]{:S(2)}, u32[]{:S(2)}) collective-permute-start(f32[128,256]{1,0:T(8,128)S(1)} %fusion.11), channel_id=1, source_target_pairs={{0,2},{1,3},{2,0},{3,1},{4,6},{5,7},{6,4},{7,5},{8,10},{9,11},{10,... | collective-permute-start | bytes 393224 | tf_op jit(solution)/shard_map/ppermute | solution.py:43
